TPU v7x, 512 devices: a whole 4x8x8 slice. The times are simulated.
512 devices in a mesh: seq: 8 (over z_lo, core), ctx: 64 (over z_hi, y, x).
Axes of the slice: x: 4, y: 8, z: 8 (z_hi: 2, z_lo: 4; z = z_hi * 4 + z_lo), core: 2. Of those that a mesh axis runs over, the one named last changes fastest.
Arguments:
- tokens: bfloat16 [8, 8192, 2048], P('seq', 'ctx'), may hold values from -80 to 80
- qkv_weight: bfloat16 [2048, 1536], P(None, 'seq'), may hold values from -0.125 to 0.125
- doc_lengths: int32 [8, 36], P('seq'), may hold values from 1 to 1024, 8192 in all within a row
- span_order: int32 [8, 128], P('seq'), may hold values from 0 to 127, as said below
Outputs:
- attended: bfloat16 [8, 8192, 1024], P('seq', 'ctx')
Inputs may be any that keep to these rules, and one draw needn't show every extreme that they name: `doc_lengths`: each row sums to 8192; its largest entry is exactly 1024. `span_order`: in each row, slots 2 i and 2 i + 1 hold spans i and 127 - i, in an order drawn for each pair.
All inputs are finite; a program needn't handle non-finite values.
Results may differ from a plain program's by a relative error of at most 0.012.
The roundings to bfloat16 on the way count: a program that leaves them out, or rounds other values in their place, can miss the bound.
Values may be sent and summed in bfloat16 or wider, within the bound.
No kernel may reach another device: no remote copies, remote signals or barrier semaphores. Data moves between devices by JAX's collectives and lax.ppermute only.
A program may use at most 192 MiB of HBM per device.

v0:
```python
import jax
import jax.numpy as jnp
from jax import lax
from jax.sharding import PartitionSpec as P

QUERY_HEADS = 16
KEY_VALUE_HEADS = 4
HEAD_SIZE = 64
QUERY_PER_KV = 4
SPAN = 64


def shifted(value, axis, steps):
    count = lax.axis_size(axis)
    initial, last = (max(0, -steps), min(count, count - steps))
    return lax.ppermute(value, axis, [(source, source + steps) for source in range(initial, last)])


def apply_rotary(value_rows, token_positions):
    token_count = value_rows.shape[0]
    heads = value_rows.reshape(token_count, -1, HEAD_SIZE)
    half = HEAD_SIZE // 2
    freq = 500000.0 ** (-jnp.arange(half, dtype=jnp.float32) * 2.0 / HEAD_SIZE)
    angle = token_positions.astype(jnp.float32)[:, None] * freq[None, :]
    cosine = jnp.cos(angle)[:, None, :]
    sine = jnp.sin(angle)[:, None, :]
    first = heads[..., :half]
    second = heads[..., half:]
    turned = jnp.concatenate(
        [first * cosine - second * sine, second * cosine + first * sine], axis=-1
    )
    return turned.reshape(token_count, -1)


def positions(order_row):
    offsets = jnp.arange(SPAN, dtype=jnp.int32)
    return (order_row[:, None] * SPAN + offsets[None, :]).reshape(-1)


def documents(lengths_row, token_positions):
    ends = jnp.cumsum(lengths_row)
    return jnp.sum((ends[None, :] <= token_positions[:, None]).astype(jnp.int32), axis=1)


def body(tokens, qkv_weight, doc_lengths, span_order):
    rows = tokens[0]
    token_count = rows.shape[0]
    query_key_value = jnp.dot(
        rows,
        lax.all_gather(qkv_weight, "seq", axis=1, tiled=True),
        preferred_element_type=jnp.float32,
    ).astype(jnp.bfloat16)
    lengths_row = doc_lengths[0]
    order_row = span_order[0]
    places_all = positions(order_row)
    docs_all = documents(lengths_row, places_all)
    my_index = lax.axis_index("ctx")
    first_row = my_index * token_count
    token_positions = lax.dynamic_slice_in_dim(places_all, first_row, token_count)
    docs = lax.dynamic_slice_in_dim(docs_all, first_row, token_count)
    query_rows = apply_rotary(
        query_key_value[:, : QUERY_HEADS * HEAD_SIZE].astype(jnp.float32), token_positions
    ).astype(jnp.bfloat16)
    key_rows = apply_rotary(
        query_key_value[
            :, QUERY_HEADS * HEAD_SIZE : (QUERY_HEADS + KEY_VALUE_HEADS) * HEAD_SIZE
        ].astype(jnp.float32),
        token_positions,
    ).astype(jnp.bfloat16)
    value_rows = query_key_value[:, (QUERY_HEADS + KEY_VALUE_HEADS) * HEAD_SIZE :]
    query_head_rows = query_rows.reshape(token_count, KEY_VALUE_HEADS, QUERY_PER_KV, HEAD_SIZE)

    def absorb_block(carry, key_block_part, value_block_part, key_places, key_docs, usable):
        block_rows = key_block_part.shape[0]
        live = (
            (docs[:, None] == key_docs[None, :])
            & (key_places[None, :] <= token_positions[:, None])
            & usable
        )
        running_state, total, summed = carry
        key_head_rows = key_block_part.reshape(block_rows, KEY_VALUE_HEADS, HEAD_SIZE)
        value_head_rows = value_block_part.reshape(block_rows, KEY_VALUE_HEADS, HEAD_SIZE)
        scores = (
            jnp.einsum(
                "qhgd,khd->hgqk", query_head_rows, key_head_rows, preferred_element_type=jnp.float32
            )
            * 0.125
        )
        scores = jnp.where(live, scores, -1e30)
        newest = jnp.maximum(running_state, jnp.max(scores, axis=-1))
        factor = jnp.exp(running_state - newest)
        weights = jnp.where(live, jnp.exp(scores - newest[..., None]), 0.0)
        total = total * factor + jnp.sum(weights, axis=-1)
        added = jnp.einsum(
            "hgqk,khd->hgqd",
            weights.astype(jnp.bfloat16),
            value_head_rows,
            preferred_element_type=jnp.float32,
        )
        summed = summed * factor[..., None] + added
        return (newest, total, summed)

    initial = (
        jnp.full((KEY_VALUE_HEADS, QUERY_PER_KV, token_count), -1e30, jnp.float32),
        jnp.zeros((KEY_VALUE_HEADS, QUERY_PER_KV, token_count), jnp.float32),
        jnp.zeros((KEY_VALUE_HEADS, QUERY_PER_KV, token_count, HEAD_SIZE), jnp.float32),
    )
    devices = lax.axis_size("ctx")
    key_cols = key_rows.shape[1]
    stacked = jnp.concatenate([key_rows, value_rows], axis=1)
    early_first = order_row[2 * my_index] < devices
    offset = jnp.where(early_first, 0, SPAN).astype(jnp.int32)
    early_rows = lax.dynamic_slice_in_dim(stacked, offset, SPAN, 0)
    late_rows = lax.dynamic_slice_in_dim(stacked, SPAN - offset, SPAN, 0)
    pair_rows = jnp.concatenate([early_rows, late_rows], axis=0)
    ramp = jnp.arange(SPAN, dtype=jnp.int32)
    state = absorb_block(initial, key_rows, value_rows, token_positions, docs, jnp.array(True))

    def advance(step, loop_state):
        carry, upward, downward = loop_state
        upward = shifted(upward, "ctx", 1)
        downward = shifted(downward, "ctx", -1)
        lower = my_index - step
        upper = my_index + step
        up_places = lower * SPAN + ramp
        carry = absorb_block(
            carry,
            upward[:, :key_cols],
            upward[:, key_cols:],
            up_places,
            documents(lengths_row, up_places),
            lower >= 0,
        )
        down_places = jnp.concatenate(
            [upper * SPAN + ramp, (2 * devices - 1 - upper) * SPAN + ramp]
        )
        carry = absorb_block(
            carry,
            downward[:, :key_cols],
            downward[:, key_cols:],
            down_places,
            documents(lengths_row, down_places),
            upper < devices,
        )
        return (carry, upward, downward)

    final_state = lax.fori_loop(1, devices // 4 + 1, advance, (state, early_rows, pair_rows))
    running_state, total, summed = final_state[0]
    outputs = summed / total[..., None]
    outputs = (
        jnp.transpose(outputs, (2, 0, 1, 3))
        .reshape(token_count, QUERY_HEADS * HEAD_SIZE)
        .astype(jnp.bfloat16)
    )
    return outputs[None]


def solution(mesh):
    placed = (P("seq", "ctx", None), P(None, "seq"), P("seq", None), P("seq", None))
    return jax.shard_map(
        body, mesh=mesh, in_specs=placed, out_specs=P("seq", "ctx", None), check_vma=False
    )
```

profile of v0, /device:TPU:448, one launch (start us, length us, event | category | flops | bytes accessed | tf_op | source)
XLA Modules:
  0.0 397.3 jit_solution(10987647458740105769)
XLA Ops:
  12.5 69.8 %all-gather.2.cloned.1.call-done = bf16[2048,1536]{0,1:T(8,128)(2,1)} async-done(((bf16[2048,192]{0,1:T(8,128)(2,1)}), bf16[2048,1536]{0,1:T(8,128)(2,1)}) %all-gather.2.cloned.1.call-update) | async-done | bytes 6291472 | tf_op jit(solution)/shard_map/all_gather | solution.py:50
  82.3 5.0 %convolution_convert_fusion = bf16[128,1536]{1,0:T(8,128)(2,1)S(1)} fusion(bf16[2048,1536]{0,1:T(8,128)(2,1)} %all-gather.2.cloned.1.call-done, bf16[1,128,2048]{2,1,0:T(8,128)(2,1)S(1)} %copy-done), kind=kOutput, calls=%fused_computation.36 | convolution fusion | flops 805502976 | bytes 7208960 | tf_op jit(solution)/shard_map/dot_general | solution.py:48
  89.2 300.4 %while.25 = (s32[]{:T(128)}, f32[4,4,128]{2,1,0:T(4,128)S(1)}, f32[4,4,128]{2,1,0:T(4,128)S(1)}, f32[4,4,128,64]{2,3,1,0:T(8,128)S(1)}, bf16[64,512]{1,0:T(8,128...) while((s32[]{:T(128)}, f32[4,4,128]{2,1,0:T(4,128)S(1)}, ...), condition=%wide.region_12.13_spmd.clone.clone, body=%wide.region_5.12_spmd.clone.clone.sunk | while | flops 104853896 | bytes 9559397 | solution.py:147
  89.2 9.7 %collective-permute-start = (bf16[128,512]{0,1:T(8,128)(2,1)S(1)}, bf16[128,512]{0,1:T(8,128)(2,1)S(1)}, u32[]{:S(2)}, u32[]{:S(2)}) collective-permute-start(bf16[128,512]{0,1:T(8,128)(2,1)S(1)} %get-tuple-element.555), channel_id=1, source_target_pairs={{1,0},{2,1},{3,2},{4,3},{5,4},{6,5},{7,6},{8,7},{9,8},{10,9},{11,1... | collective-permute-start | bytes 393224 | tf_op jit(solution)/shard_map/while/body/eval_jaxpr/ppermute | solution.py:16
  101.3 11.9 %collective-permute-done.1 = bf16[64,512]{1,0:T(8,128)(2,1)S(1)} collective-permute-done((bf16[64,512]{1,0:T(8,128)(2,1)S(1)}, bf16[64,512]{1,0:T(8,128)(2,1)S(1)}, u32[]{:S(2)}, u32[]{:S(2)}) %collective-permute-start.1) | collective-permute-done | bytes 65568 | tf_op jit(solution)/shard_map/while/body/eval_jaxpr/ppermute | solution.py:16
  116.9 3.9 collective-permute-start.1
  121.4 9.9 %collective-permute-done.1 = bf16[64,512]{1,0:T(8,128)(2,1)S(1)} collective-permute-done((bf16[64,512]{1,0:T(8,128)(2,1)S(1)}, bf16[64,512]{1,0:T(8,128)(2,1)S(1)}, u32[]{:S(2)}, u32[]{:S(2)}) %collective-permute-start.1) | collective-permute-done | bytes 65568 | tf_op jit(solution)/shard_map/while/body/eval_jaxpr/ppermute | solution.py:16
  139.4 10.4 %collective-permute-done.1 = bf16[64,512]{1,0:T(8,128)(2,1)S(1)} collective-permute-done((bf16[64,512]{1,0:T(8,128)(2,1)S(1)}, bf16[64,512]{1,0:T(8,128)(2,1)S(1)}, u32[]{:S(2)}, u32[]{:S(2)}) %collective-permute-start.1) | collective-permute-done | bytes 65568 | tf_op jit(solution)/shard_map/while/body/eval_jaxpr/ppermute | solution.py:16
  153.6 3.9 collective-permute-start.1
  158.0 10.0 %collective-permute-done.1 = bf16[64,512]{1,0:T(8,128)(2,1)S(1)} collective-permute-done((bf16[64,512]{1,0:T(8,128)(2,1)S(1)}, bf16[64,512]{1,0:T(8,128)(2,1)S(1)}, u32[]{:S(2)}, u32[]{:S(2)}) %collective-permute-start.1) | collective-permute-done | bytes 65568 | tf_op jit(solution)/shard_map/while/body/eval_jaxpr/ppermute | solution.py:16
  171.7 3.9 collective-permute-start.1
  176.2 10.0 %collective-permute-done.1 = bf16[64,512]{1,0:T(8,128)(2,1)S(1)} collective-permute-done((bf16[64,512]{1,0:T(8,128)(2,1)S(1)}, bf16[64,512]{1,0:T(8,128)(2,1)S(1)}, u32[]{:S(2)}, u32[]{:S(2)}) %collective-permute-start.1) | collective-permute-done | bytes 65568 | tf_op jit(solution)/shard_map/while/body/eval_jaxpr/ppermute | solution.py:16
  189.9 3.9 collective-permute-start.1
  194.3 10.0 %collective-permute-done.1 = bf16[64,512]{1,0:T(8,128)(2,1)S(1)} collective-permute-done((bf16[64,512]{1,0:T(8,128)(2,1)S(1)}, bf16[64,512]{1,0:T(8,128)(2,1)S(1)}, u32[]{:S(2)}, u32[]{:S(2)}) %collective-permute-start.1) | collective-permute-done | bytes 65568 | tf_op jit(solution)/shard_map/while/body/eval_jaxpr/ppermute | solution.py:16
  208.1 3.9 collective-permute-start.1
  212.5 10.0 %collective-permute-done.1 = bf16[64,512]{1,0:T(8,128)(2,1)S(1)} collective-permute-done((bf16[64,512]{1,0:T(8,128)(2,1)S(1)}, bf16[64,512]{1,0:T(8,128)(2,1)S(1)}, u32[]{:S(2)}, u32[]{:S(2)}) %collective-permute-start.1) | collective-permute-done | bytes 65568 | tf_op jit(solution)/shard_map/while/body/eval_jaxpr/ppermute | solution.py:16
  226.3 3.9 collective-permute-start.1
  230.7 10.0 %collective-permute-done.1 = bf16[64,512]{1,0:T(8,128)(2,1)S(1)} collective-permute-done((bf16[64,512]{1,0:T(8,128)(2,1)S(1)}, bf16[64,512]{1,0:T(8,128)(2,1)S(1)}, u32[]{:S(2)}, u32[]{:S(2)}) %collective-permute-start.1) | collective-permute-done | bytes 65568 | tf_op jit(solution)/shard_map/while/body/eval_jaxpr/ppermute | solution.py:16
  244.4 3.9 collective-permute-start.1
  248.9 10.0 %collective-permute-done.1 = bf16[64,512]{1,0:T(8,128)(2,1)S(1)} collective-permute-done((bf16[64,512]{1,0:T(8,128)(2,1)S(1)}, bf16[64,512]{1,0:T(8,128)(2,1)S(1)}, u32[]{:S(2)}, u32[]{:S(2)}) %collective-permute-start.1) | collective-permute-done | bytes 65568 | tf_op jit(solution)/shard_map/while/body/eval_jaxpr/ppermute | solution.py:16
  262.6 3.9 collective-permute-start.1
  267.0 10.0 %collective-permute-done.1 = bf16[64,512]{1,0:T(8,128)(2,1)S(1)} collective-permute-done((bf16[64,512]{1,0:T(8,128)(2,1)S(1)}, bf16[64,512]{1,0:T(8,128)(2,1)S(1)}, u32[]{:S(2)}, u32[]{:S(2)}) %collective-permute-start.1) | collective-permute-done | bytes 65568 | tf_op jit(solution)/shard_map/while/body/eval_jaxpr/ppermute | solution.py:16
  280.8 3.9 collective-permute-start.1
  285.2 10.0 %collective-permute-done.1 = bf16[64,512]{1,0:T(8,128)(2,1)S(1)} collective-permute-done((bf16[64,512]{1,0:T(8,128)(2,1)S(1)}, bf16[64,512]{1,0:T(8,128)(2,1)S(1)}, u32[]{:S(2)}, u32[]{:S(2)}) %collective-permute-start.1) | collective-permute-done | bytes 65568 | tf_op jit(solution)/shard_map/while/body/eval_jaxpr/ppermute | solution.py:16
  299.0 3.9 collective-permute-start.1
  303.4 10.0 %collective-permute-done.1 = bf16[64,512]{1,0:T(8,128)(2,1)S(1)} collective-permute-done((bf16[64,512]{1,0:T(8,128)(2,1)S(1)}, bf16[64,512]{1,0:T(8,128)(2,1)S(1)}, u32[]{:S(2)}, u32[]{:S(2)}) %collective-permute-start.1) | collective-permute-done | bytes 65568 | tf_op jit(solution)/shard_map/while/body/eval_jaxpr/ppermute | solution.py:16
  317.1 3.9 collective-permute-start.1
  321.6 10.0 %collective-permute-done.1 = bf16[64,512]{1,0:T(8,128)(2,1)S(1)} collective-permute-done((bf16[64,512]{1,0:T(8,128)(2,1)S(1)}, bf16[64,512]{1,0:T(8,128)(2,1)S(1)}, u32[]{:S(2)}, u32[]{:S(2)}) %collective-permute-start.1) | collective-permute-done | bytes 65568 | tf_op jit(solution)/shard_map/while/body/eval_jaxpr/ppermute | solution.py:16
  335.3 3.9 collective-permute-start.1
  339.7 11.2 %collective-permute-done.1 = bf16[64,512]{1,0:T(8,128)(2,1)S(1)} collective-permute-done((bf16[64,512]{1,0:T(8,128)(2,1)S(1)}, bf16[64,512]{1,0:T(8,128)(2,1)S(1)}, u32[]{:S(2)}, u32[]{:S(2)}) %collective-permute-start.1) | collective-permute-done | bytes 65568 | tf_op jit(solution)/shard_map/while/body/eval_jaxpr/ppermute | solution.py:16
  359.2 10.1 %collective-permute-done.1 = bf16[64,512]{1,0:T(8,128)(2,1)S(1)} collective-permute-done((bf16[64,512]{1,0:T(8,128)(2,1)S(1)}, bf16[64,512]{1,0:T(8,128)(2,1)S(1)}, u32[]{:S(2)}, u32[]{:S(2)}) %collective-permute-start.1) | collective-permute-done | bytes 65568 | tf_op jit(solution)/shard_map/while/body/eval_jaxpr/ppermute | solution.py:16
  377.5 10.2 %collective-permute-done.1 = bf16[64,512]{1,0:T(8,128)(2,1)S(1)} collective-permute-done((bf16[64,512]{1,0:T(8,128)(2,1)S(1)}, bf16[64,512]{1,0:T(8,128)(2,1)S(1)}, u32[]{:S(2)}, u32[]{:S(2)}) %collective-permute-start.1) | collective-permute-done | bytes 65568 | tf_op jit(solution)/shard_map/while/body/eval_jaxpr/ppermute | solution.py:16
  (425 shorter events, 85.4 us)
Async XLA Ops:
  6.5 75.8 %all-gather.2.cloned.1.call-start = ((), (), s32[]{:S(2)}) async-start(), calls=%async_computation | async-start | bytes 7077888 | tf_op jit(solution)/shard_map/all_gather | solution.py:50
  89.2 24.5 %collective-permute-start = (bf16[128,512]{0,1:T(8,128)(2,1)S(1)}, bf16[128,512]{0,1:T(8,128)(2,1)S(1)}, u32[]{:S(2)}, u32[]{:S(2)}) collective-permute-start(bf16[128,512]{0,1:T(8,128)(2,1)S(1)} %get-tuple-element.555), channel_id=1, source_target_pairs={{1,0},{2,1},{3,2},{4,3},{5,4},{6,5},{7,6},{8,7},{9,8},{10,9},{11,1... | collective-permute-start | bytes 393224 | tf_op jit(solution)/shard_map/while/body/eval_jaxpr/ppermute | solution.py:16
  98.9 14.3 %collective-permute-start.1 = (bf16[64,512]{1,0:T(8,128)(2,1)S(1)}, bf16[64,512]{1,0:T(8,128)(2,1)S(1)}, u32[]{:S(2)}, u32[]{:S(2)}) collective-permute-start(bf16[64,512]{1,0:T(8,128)(2,1)S(1)} %get-tuple-element.554), channel_id=1, source_target_pairs={{0,1},{1,2},{2,3},{3,4},{4,5},{5,6},{6,7},{7,8},{8,9},{9,10},{10,1... | collective-permute-start | bytes 196616 | tf_op jit(solution)/shard_map/while/body/eval_jaxpr/ppermute | solution.py:16
  115.0 16.7 %collective-permute-start = (bf16[128,512]{0,1:T(8,128)(2,1)S(1)}, bf16[128,512]{0,1:T(8,128)(2,1)S(1)}, u32[]{:S(2)}, u32[]{:S(2)}) collective-permute-start(bf16[128,512]{0,1:T(8,128)(2,1)S(1)} %get-tuple-element.555), channel_id=1, source_target_pairs={{1,0},{2,1},{3,2},{4,3},{5,4},{6,5},{7,6},{8,7},{9,8},{10,9},{11,1... | collective-permute-start | bytes 393224 | tf_op jit(solution)/shard_map/while/body/eval_jaxpr/ppermute | solution.py:16
  116.9 14.3 %collective-permute-start.1 = (bf16[64,512]{1,0:T(8,128)(2,1)S(1)}, bf16[64,512]{1,0:T(8,128)(2,1)S(1)}, u32[]{:S(2)}, u32[]{:S(2)}) collective-permute-start(bf16[64,512]{1,0:T(8,128)(2,1)S(1)} %get-tuple-element.554), channel_id=1, source_target_pairs={{0,1},{1,2},{2,3},{3,4},{4,5},{5,6},{6,7},{7,8},{8,9},{9,10},{10,1... | collective-permute-start | bytes 196616 | tf_op jit(solution)/shard_map/while/body/eval_jaxpr/ppermute | solution.py:16
  133.0 17.3 %collective-permute-start = (bf16[128,512]{0,1:T(8,128)(2,1)S(1)}, bf16[128,512]{0,1:T(8,128)(2,1)S(1)}, u32[]{:S(2)}, u32[]{:S(2)}) collective-permute-start(bf16[128,512]{0,1:T(8,128)(2,1)S(1)} %get-tuple-element.555), channel_id=1, source_target_pairs={{1,0},{2,1},{3,2},{4,3},{5,4},{6,5},{7,6},{8,7},{9,8},{10,9},{11,1... | collective-permute-start | bytes 393224 | tf_op jit(solution)/shard_map/while/body/eval_jaxpr/ppermute | solution.py:16
  135.4 14.4 %collective-permute-start.1 = (bf16[64,512]{1,0:T(8,128)(2,1)S(1)}, bf16[64,512]{1,0:T(8,128)(2,1)S(1)}, u32[]{:S(2)}, u32[]{:S(2)}) collective-permute-start(bf16[64,512]{1,0:T(8,128)(2,1)S(1)} %get-tuple-element.554), channel_id=1, source_target_pairs={{0,1},{1,2},{2,3},{3,4},{4,5},{5,6},{6,7},{7,8},{8,9},{9,10},{10,1... | collective-permute-start | bytes 196616 | tf_op jit(solution)/shard_map/while/body/eval_jaxpr/ppermute | solution.py:16
  151.7 16.8 %collective-permute-start = (bf16[128,512]{0,1:T(8,128)(2,1)S(1)}, bf16[128,512]{0,1:T(8,128)(2,1)S(1)}, u32[]{:S(2)}, u32[]{:S(2)}) collective-permute-start(bf16[128,512]{0,1:T(8,128)(2,1)S(1)} %get-tuple-element.555), channel_id=1, source_target_pairs={{1,0},{2,1},{3,2},{4,3},{5,4},{6,5},{7,6},{8,7},{9,8},{10,9},{11,1... | collective-permute-start | bytes 393224 | tf_op jit(solution)/shard_map/while/body/eval_jaxpr/ppermute | solution.py:16
  153.6 14.4 %collective-permute-start.1 = (bf16[64,512]{1,0:T(8,128)(2,1)S(1)}, bf16[64,512]{1,0:T(8,128)(2,1)S(1)}, u32[]{:S(2)}, u32[]{:S(2)}) collective-permute-start(bf16[64,512]{1,0:T(8,128)(2,1)S(1)} %get-tuple-element.554), channel_id=1, source_target_pairs={{0,1},{1,2},{2,3},{3,4},{4,5},{5,6},{6,7},{7,8},{8,9},{9,10},{10,1... | collective-permute-start | bytes 196616 | tf_op jit(solution)/shard_map/while/body/eval_jaxpr/ppermute | solution.py:16
  169.8 16.8 %collective-permute-start = (bf16[128,512]{0,1:T(8,128)(2,1)S(1)}, bf16[128,512]{0,1:T(8,128)(2,1)S(1)}, u32[]{:S(2)}, u32[]{:S(2)}) collective-permute-start(bf16[128,512]{0,1:T(8,128)(2,1)S(1)} %get-tuple-element.555), channel_id=1, source_target_pairs={{1,0},{2,1},{3,2},{4,3},{5,4},{6,5},{7,6},{8,7},{9,8},{10,9},{11,1... | collective-permute-start | bytes 393224 | tf_op jit(solution)/shard_map/while/body/eval_jaxpr/ppermute | solution.py:16
  171.7 14.4 %collective-permute-start.1 = (bf16[64,512]{1,0:T(8,128)(2,1)S(1)}, bf16[64,512]{1,0:T(8,128)(2,1)S(1)}, u32[]{:S(2)}, u32[]{:S(2)}) collective-permute-start(bf16[64,512]{1,0:T(8,128)(2,1)S(1)} %get-tuple-element.554), channel_id=1, source_target_pairs={{0,1},{1,2},{2,3},{3,4},{4,5},{5,6},{6,7},{7,8},{8,9},{9,10},{10,1... | collective-permute-start | bytes 196616 | tf_op jit(solution)/shard_map/while/body/eval_jaxpr/ppermute | solution.py:16
  188.0 16.8 %collective-permute-start = (bf16[128,512]{0,1:T(8,128)(2,1)S(1)}, bf16[128,512]{0,1:T(8,128)(2,1)S(1)}, u32[]{:S(2)}, u32[]{:S(2)}) collective-permute-start(bf16[128,512]{0,1:T(8,128)(2,1)S(1)} %get-tuple-element.555), channel_id=1, source_target_pairs={{1,0},{2,1},{3,2},{4,3},{5,4},{6,5},{7,6},{8,7},{9,8},{10,9},{11,1... | collective-permute-start | bytes 393224 | tf_op jit(solution)/shard_map/while/body/eval_jaxpr/ppermute | solution.py:16
  189.9 14.4 %collective-permute-start.1 = (bf16[64,512]{1,0:T(8,128)(2,1)S(1)}, bf16[64,512]{1,0:T(8,128)(2,1)S(1)}, u32[]{:S(2)}, u32[]{:S(2)}) collective-permute-start(bf16[64,512]{1,0:T(8,128)(2,1)S(1)} %get-tuple-element.554), channel_id=1, source_target_pairs={{0,1},{1,2},{2,3},{3,4},{4,5},{5,6},{6,7},{7,8},{8,9},{9,10},{10,1... | collective-permute-start | bytes 196616 | tf_op jit(solution)/shard_map/while/body/eval_jaxpr/ppermute | solution.py:16
  206.2 16.8 %collective-permute-start = (bf16[128,512]{0,1:T(8,128)(2,1)S(1)}, bf16[128,512]{0,1:T(8,128)(2,1)S(1)}, u32[]{:S(2)}, u32[]{:S(2)}) collective-permute-start(bf16[128,512]{0,1:T(8,128)(2,1)S(1)} %get-tuple-element.555), channel_id=1, source_target_pairs={{1,0},{2,1},{3,2},{4,3},{5,4},{6,5},{7,6},{8,7},{9,8},{10,9},{11,1... | collective-permute-start | bytes 393224 | tf_op jit(solution)/shard_map/while/body/eval_jaxpr/ppermute | solution.py:16
  208.1 14.4 %collective-permute-start.1 = (bf16[64,512]{1,0:T(8,128)(2,1)S(1)}, bf16[64,512]{1,0:T(8,128)(2,1)S(1)}, u32[]{:S(2)}, u32[]{:S(2)}) collective-permute-start(bf16[64,512]{1,0:T(8,128)(2,1)S(1)} %get-tuple-element.554), channel_id=1, source_target_pairs={{0,1},{1,2},{2,3},{3,4},{4,5},{5,6},{6,7},{7,8},{8,9},{9,10},{10,1... | collective-permute-start | bytes 196616 | tf_op jit(solution)/shard_map/while/body/eval_jaxpr/ppermute | solution.py:16
  224.3 16.8 %collective-permute-start = (bf16[128,512]{0,1:T(8,128)(2,1)S(1)}, bf16[128,512]{0,1:T(8,128)(2,1)S(1)}, u32[]{:S(2)}, u32[]{:S(2)}) collective-permute-start(bf16[128,512]{0,1:T(8,128)(2,1)S(1)} %get-tuple-element.555), channel_id=1, source_target_pairs={{1,0},{2,1},{3,2},{4,3},{5,4},{6,5},{7,6},{8,7},{9,8},{10,9},{11,1... | collective-permute-start | bytes 393224 | tf_op jit(solution)/shard_map/while/body/eval_jaxpr/ppermute | solution.py:16
  226.3 14.4 %collective-permute-start.1 = (bf16[64,512]{1,0:T(8,128)(2,1)S(1)}, bf16[64,512]{1,0:T(8,128)(2,1)S(1)}, u32[]{:S(2)}, u32[]{:S(2)}) collective-permute-start(bf16[64,512]{1,0:T(8,128)(2,1)S(1)} %get-tuple-element.554), channel_id=1, source_target_pairs={{0,1},{1,2},{2,3},{3,4},{4,5},{5,6},{6,7},{7,8},{8,9},{9,10},{10,1... | collective-permute-start | bytes 196616 | tf_op jit(solution)/shard_map/while/body/eval_jaxpr/ppermute | solution.py:16
  242.5 16.8 %collective-permute-start = (bf16[128,512]{0,1:T(8,128)(2,1)S(1)}, bf16[128,512]{0,1:T(8,128)(2,1)S(1)}, u32[]{:S(2)}, u32[]{:S(2)}) collective-permute-start(bf16[128,512]{0,1:T(8,128)(2,1)S(1)} %get-tuple-element.555), channel_id=1, source_target_pairs={{1,0},{2,1},{3,2},{4,3},{5,4},{6,5},{7,6},{8,7},{9,8},{10,9},{11,1... | collective-permute-start | bytes 393224 | tf_op jit(solution)/shard_map/while/body/eval_jaxpr/ppermute | solution.py:16
  244.4 14.4 %collective-permute-start.1 = (bf16[64,512]{1,0:T(8,128)(2,1)S(1)}, bf16[64,512]{1,0:T(8,128)(2,1)S(1)}, u32[]{:S(2)}, u32[]{:S(2)}) collective-permute-start(bf16[64,512]{1,0:T(8,128)(2,1)S(1)} %get-tuple-element.554), channel_id=1, source_target_pairs={{0,1},{1,2},{2,3},{3,4},{4,5},{5,6},{6,7},{7,8},{8,9},{9,10},{10,1... | collective-permute-start | bytes 196616 | tf_op jit(solution)/shard_map/while/body/eval_jaxpr/ppermute | solution.py:16
  260.7 16.8 %collective-permute-start = (bf16[128,512]{0,1:T(8,128)(2,1)S(1)}, bf16[128,512]{0,1:T(8,128)(2,1)S(1)}, u32[]{:S(2)}, u32[]{:S(2)}) collective-permute-start(bf16[128,512]{0,1:T(8,128)(2,1)S(1)} %get-tuple-element.555), channel_id=1, source_target_pairs={{1,0},{2,1},{3,2},{4,3},{5,4},{6,5},{7,6},{8,7},{9,8},{10,9},{11,1... | collective-permute-start | bytes 393224 | tf_op jit(solution)/shard_map/while/body/eval_jaxpr/ppermute | solution.py:16
  262.6 14.4 %collective-permute-start.1 = (bf16[64,512]{1,0:T(8,128)(2,1)S(1)}, bf16[64,512]{1,0:T(8,128)(2,1)S(1)}, u32[]{:S(2)}, u32[]{:S(2)}) collective-permute-start(bf16[64,512]{1,0:T(8,128)(2,1)S(1)} %get-tuple-element.554), channel_id=1, source_target_pairs={{0,1},{1,2},{2,3},{3,4},{4,5},{5,6},{6,7},{7,8},{8,9},{9,10},{10,1... | collective-permute-start | bytes 196616 | tf_op jit(solution)/shard_map/while/body/eval_jaxpr/ppermute | solution.py:16
  278.9 16.8 %collective-permute-start = (bf16[128,512]{0,1:T(8,128)(2,1)S(1)}, bf16[128,512]{0,1:T(8,128)(2,1)S(1)}, u32[]{:S(2)}, u32[]{:S(2)}) collective-permute-start(bf16[128,512]{0,1:T(8,128)(2,1)S(1)} %get-tuple-element.555), channel_id=1, source_target_pairs={{1,0},{2,1},{3,2},{4,3},{5,4},{6,5},{7,6},{8,7},{9,8},{10,9},{11,1... | collective-permute-start | bytes 393224 | tf_op jit(solution)/shard_map/while/body/eval_jaxpr/ppermute | solution.py:16
  280.8 14.4 %collective-permute-start.1 = (bf16[64,512]{1,0:T(8,128)(2,1)S(1)}, bf16[64,512]{1,0:T(8,128)(2,1)S(1)}, u32[]{:S(2)}, u32[]{:S(2)}) collective-permute-start(bf16[64,512]{1,0:T(8,128)(2,1)S(1)} %get-tuple-element.554), channel_id=1, source_target_pairs={{0,1},{1,2},{2,3},{3,4},{4,5},{5,6},{6,7},{7,8},{8,9},{9,10},{10,1... | collective-permute-start | bytes 196616 | tf_op jit(solution)/shard_map/while/body/eval_jaxpr/ppermute | solution.py:16
  297.0 16.8 %collective-permute-start = (bf16[128,512]{0,1:T(8,128)(2,1)S(1)}, bf16[128,512]{0,1:T(8,128)(2,1)S(1)}, u32[]{:S(2)}, u32[]{:S(2)}) collective-permute-start(bf16[128,512]{0,1:T(8,128)(2,1)S(1)} %get-tuple-element.555), channel_id=1, source_target_pairs={{1,0},{2,1},{3,2},{4,3},{5,4},{6,5},{7,6},{8,7},{9,8},{10,9},{11,1... | collective-permute-start | bytes 393224 | tf_op jit(solution)/shard_map/while/body/eval_jaxpr/ppermute | solution.py:16
  299.0 14.4 %collective-permute-start.1 = (bf16[64,512]{1,0:T(8,128)(2,1)S(1)}, bf16[64,512]{1,0:T(8,128)(2,1)S(1)}, u32[]{:S(2)}, u32[]{:S(2)}) collective-permute-start(bf16[64,512]{1,0:T(8,128)(2,1)S(1)} %get-tuple-element.554), channel_id=1, source_target_pairs={{0,1},{1,2},{2,3},{3,4},{4,5},{5,6},{6,7},{7,8},{8,9},{9,10},{10,1... | collective-permute-start | bytes 196616 | tf_op jit(solution)/shard_map/while/body/eval_jaxpr/ppermute | solution.py:16
  315.2 16.8 %collective-permute-start = (bf16[128,512]{0,1:T(8,128)(2,1)S(1)}, bf16[128,512]{0,1:T(8,128)(2,1)S(1)}, u32[]{:S(2)}, u32[]{:S(2)}) collective-permute-start(bf16[128,512]{0,1:T(8,128)(2,1)S(1)} %get-tuple-element.555), channel_id=1, source_target_pairs={{1,0},{2,1},{3,2},{4,3},{5,4},{6,5},{7,6},{8,7},{9,8},{10,9},{11,1... | collective-permute-start | bytes 393224 | tf_op jit(solution)/shard_map/while/body/eval_jaxpr/ppermute | solution.py:16
  317.1 14.4 %collective-permute-start.1 = (bf16[64,512]{1,0:T(8,128)(2,1)S(1)}, bf16[64,512]{1,0:T(8,128)(2,1)S(1)}, u32[]{:S(2)}, u32[]{:S(2)}) collective-permute-start(bf16[64,512]{1,0:T(8,128)(2,1)S(1)} %get-tuple-element.554), channel_id=1, source_target_pairs={{0,1},{1,2},{2,3},{3,4},{4,5},{5,6},{6,7},{7,8},{8,9},{9,10},{10,1... | collective-permute-start | bytes 196616 | tf_op jit(solution)/shard_map/while/body/eval_jaxpr/ppermute | solution.py:16
  333.4 18.1 %collective-permute-start = (bf16[128,512]{0,1:T(8,128)(2,1)S(1)}, bf16[128,512]{0,1:T(8,128)(2,1)S(1)}, u32[]{:S(2)}, u32[]{:S(2)}) collective-permute-start(bf16[128,512]{0,1:T(8,128)(2,1)S(1)} %get-tuple-element.555), channel_id=1, source_target_pairs={{1,0},{2,1},{3,2},{4,3},{5,4},{6,5},{7,6},{8,7},{9,8},{10,9},{11,1... | collective-permute-start | bytes 393224 | tf_op jit(solution)/shard_map/while/body/eval_jaxpr/ppermute | solution.py:16
  335.3 15.7 %collective-permute-start.1 = (bf16[64,512]{1,0:T(8,128)(2,1)S(1)}, bf16[64,512]{1,0:T(8,128)(2,1)S(1)}, u32[]{:S(2)}, u32[]{:S(2)}) collective-permute-start(bf16[64,512]{1,0:T(8,128)(2,1)S(1)} %get-tuple-element.554), channel_id=1, source_target_pairs={{0,1},{1,2},{2,3},{3,4},{4,5},{5,6},{6,7},{7,8},{8,9},{9,10},{10,1... | collective-permute-start | bytes 196616 | tf_op jit(solution)/shard_map/while/body/eval_jaxpr/ppermute | solution.py:16
  352.8 17.0 %collective-permute-start = (bf16[128,512]{0,1:T(8,128)(2,1)S(1)}, bf16[128,512]{0,1:T(8,128)(2,1)S(1)}, u32[]{:S(2)}, u32[]{:S(2)}) collective-permute-start(bf16[128,512]{0,1:T(8,128)(2,1)S(1)} %get-tuple-element.555), channel_id=1, source_target_pairs={{1,0},{2,1},{3,2},{4,3},{5,4},{6,5},{7,6},{8,7},{9,8},{10,9},{11,1... | collective-permute-start | bytes 393224 | tf_op jit(solution)/shard_map/while/body/eval_jaxpr/ppermute | solution.py:16
  354.8 14.5 %collective-permute-start.1 = (bf16[64,512]{1,0:T(8,128)(2,1)S(1)}, bf16[64,512]{1,0:T(8,128)(2,1)S(1)}, u32[]{:S(2)}, u32[]{:S(2)}) collective-permute-start(bf16[64,512]{1,0:T(8,128)(2,1)S(1)} %get-tuple-element.554), channel_id=1, source_target_pairs={{0,1},{1,2},{2,3},{3,4},{4,5},{5,6},{6,7},{7,8},{8,9},{9,10},{10,1... | collective-permute-start | bytes 196616 | tf_op jit(solution)/shard_map/while/body/eval_jaxpr/ppermute | solution.py:16
  371.1 17.1 %collective-permute-start = (bf16[128,512]{0,1:T(8,128)(2,1)S(1)}, bf16[128,512]{0,1:T(8,128)(2,1)S(1)}, u32[]{:S(2)}, u32[]{:S(2)}) collective-permute-start(bf16[128,512]{0,1:T(8,128)(2,1)S(1)} %get-tuple-element.555), channel_id=1, source_target_pairs={{1,0},{2,1},{3,2},{4,3},{5,4},{6,5},{7,6},{8,7},{9,8},{10,9},{11,1... | collective-permute-start | bytes 393224 | tf_op jit(solution)/shard_map/while/body/eval_jaxpr/ppermute | solution.py:16
  (2 other events, 90.1 us)
Sparse Core Ops, SparseCore 0:
  9.4 72.8 all-gather.1
where the time goes:
time: 398 us; the launch traced here: 397 us
  waiting for transfers between devices  234 us (59%)
  starting transfers between devices  99.3 us (25%)
  matrix products  23.8 us (6%)
  other arithmetic  17 us (4%)
  between operations  14.2 us (4%)
  local copies, waits for them, and re-layouts  6.37 us (2%)
    ppermute x32, waiting for transfers between devices, shifted(): lax.ppermute(value, axis, [(source, source + steps) for source in range(i...  164 us
    ppermute x32, starting transfers between devices, shifted(): lax.ppermute(value, axis, [(source, source + steps) for source in range(i...  99.3 us
    all_gather x1, waiting for transfers between devices, body(): lax.all_gather(qkv_weight, 'seq', axis=1, tiled=True)  69.8 us
    dot_general x33, matrix products, absorb_block(): jnp.einsum('qhgd,khd->hgqk', query_head_rows, key_head_rows, preferred_el...  9.85 us
    dot_general x33, matrix products, absorb_block(): jnp.einsum('hgqk,khd->hgqd', weights.astype(jnp.bfloat16), value_head_row...  8.93 us
  transfers between devices with their start and end apart: 33, of which 17 were waited for; matrix products, arithmetic and copies ran while one was open for 5% of the time, Pallas kernels for 0%

commit v1 on v0

--- a/solution.py
+++ b/solution.py
@@ -47,7 +47,12 @@
     token_count = rows.shape[0]
     query_key_value = jnp.dot(
         rows,
-        lax.all_gather(qkv_weight, "seq", axis=1, tiled=True),
+        jnp.concatenate(
+            lax.all_to_all(
+                jnp.stack([qkv_weight for _ in range(lax.axis_size("seq"))], axis=0), "seq", 0, 0
+            ),
+            1,
+        ),
         preferred_element_type=jnp.float32,
     ).astype(jnp.bfloat16)
     lengths_row = doc_lengths[0]

time: 398 us -> 451 us (1.13)
  waiting for transfers between devices: 234 us -> 294 us
  between operations: 14.2 us -> 0.81 us
    all_to_all x0 -> x1, waiting for transfers between devices: none -> 134 us  [body(): lax.all_to_all(jnp.stack([qkv_weight for _ in range(lax.axis_size('seq'))...]
    all_gather x1 -> x0, waiting for transfers between devices: 69.8 us -> none  [body(): lax.all_gather(qkv_weight, 'seq', axis=1, tiled=True)]
    all_to_all x0 -> x1, starting transfers between devices: none -> 5.31 us  [body(): lax.all_to_all(jnp.stack([qkv_weight for _ in range(lax.axis_size('seq'))...]
  transfers between devices with their start and end apart: 33 -> 33, of which waited for: 17 -> 17; matrix products, arithmetic and copies ran while one was open for 5% -> 4% of each run, Pallas kernels for 0% -> 0%
where the time goes in v1:
time: 451 us; the launch traced here: 448 us
  waiting for transfers between devices  294 us (65%)
  starting transfers between devices  101 us (22%)
  matrix products  23.8 us (5%)
  other arithmetic  15.1 us (3%)
  local copies, waits for them, and re-layouts  10.4 us (2%)
    ppermute x32, waiting for transfers between devices, shifted(): lax.ppermute(value, axis, [(source, source + steps) for source in range(i...  160 us
    all_to_all x1, waiting for transfers between devices, body(): lax.all_to_all(jnp.stack([qkv_weight for _ in range(lax.axis_size('seq'))...  134 us
    ppermute x32, starting transfers between devices, shifted(): lax.ppermute(value, axis, [(source, source + steps) for source in range(i...  96.2 us
    dot_general x33, matrix products, absorb_block(): jnp.einsum('qhgd,khd->hgqk', query_head_rows, key_head_rows, preferred_el...  9.83 us
  transfers between devices with their start and end apart: 33, of which 17 were waited for; matrix products, arithmetic and copies ran while one was open for 4% of the time, Pallas kernels for 0%

profile of v1, /device:TPU:448, one launch (start us, length us, event | category | flops | bytes accessed | tf_op | source)
XLA Modules:
  0.0 448.2 jit_solution(392800579322837485)
XLA Ops:
  0.0 4.6 %stack.2 = bf16[8,2048,192]{1,2,0:T(8,128)(2,1)} broadcast(bf16[2048,192]{0,1:T(8,128)(2,1)} %param.7), dimensions={1,2} | broadcast | bytes 7077888 | tf_op jit(solution)/shard_map/stack | solution.py:52
  4.7 5.3 %all-to-all-start = ((bf16[8,2048,192]{1,2,0:T(8,128)(2,1)}), bf16[8,2048,192]{1,2,0:T(8,128)(2,1)}, u32[]{:S(2)}, u32[]{:S(2)}) async-start(bf16[8,2048,192]{1,2,0:T(8,128)(2,1)} %stack.2), calls=%async_computation | async-start | bytes 12582912 | tf_op jit(solution)/shard_map/all_to_all | solution.py:51
  12.6 133.8 %all-to-all-done = bf16[8,2048,192]{1,2,0:T(8,128)(2,1)} async-done(((bf16[8,2048,192]{1,2,0:T(8,128)(2,1)}), bf16[8,2048,192]{1,2,0:T(8,128)(2,1)}, u32[]{:S(2)}, u32[]{:S(2)}) %all-to-all-start) | async-done | bytes 6291488 | tf_op jit(solution)/shard_map/all_to_all | solution.py:51
  146.4 5.0 %convolution_convert_fusion = bf16[128,1536]{1,0:T(8,128)(2,1)S(1)} fusion(bf16[2048,1536]{0,1:T(8,128)(2,1)} %bitcast.4, bf16[1,128,2048]{2,1,0:T(8,128)(2,1)S(1)} %copy-done), kind=kOutput, calls=%fused_computation.36 | convolution fusion | flops 805502976 | bytes 7208960 | tf_op jit(solution)/shard_map/dot_general | solution.py:48
  153.3 294.0 %while.25 = (s32[]{:T(128)}, f32[4,4,128]{2,1,0:T(4,128)S(1)}, f32[4,4,128]{2,1,0:T(4,128)S(1)}, f32[4,4,128,64]{2,3,1,0:T(8,128)S(1)}, bf16[64,512]{1,0:T(8,128...) while((s32[]{:T(128)}, f32[4,4,128]{2,1,0:T(4,128)S(1)}, ...), condition=%wide.region_12.13_spmd.clone.clone, body=%wide.region_5.12_spmd.clone.clone.sunk | while | flops 104853896 | bytes 9559397 | solution.py:152
  153.3 6.6 %collective-permute-start = (bf16[128,512]{0,1:T(8,128)(2,1)S(1)}, bf16[128,512]{0,1:T(8,128)(2,1)S(1)}, u32[]{:S(2)}, u32[]{:S(2)}) collective-permute-start(bf16[128,512]{0,1:T(8,128)(2,1)S(1)} %get-tuple-element.555), channel_id=1, source_target_pairs={{1,0},{2,1},{3,2},{4,3},{5,4},{6,5},{7,6},{8,7},{9,8},{10,9},{11,1... | collective-permute-start | bytes 393224 | tf_op jit(solution)/shard_map/while/body/eval_jaxpr/ppermute | solution.py:16
  162.3 11.9 %collective-permute-done.1 = bf16[64,512]{1,0:T(8,128)(2,1)S(1)} collective-permute-done((bf16[64,512]{1,0:T(8,128)(2,1)S(1)}, bf16[64,512]{1,0:T(8,128)(2,1)S(1)}, u32[]{:S(2)}, u32[]{:S(2)}) %collective-permute-start.1) | collective-permute-done | bytes 65568 | tf_op jit(solution)/shard_map/while/body/eval_jaxpr/ppermute | solution.py:16
  177.9 3.9 collective-permute-start.1
  182.3 9.9 %collective-permute-done.1 = bf16[64,512]{1,0:T(8,128)(2,1)S(1)} collective-permute-done((bf16[64,512]{1,0:T(8,128)(2,1)S(1)}, bf16[64,512]{1,0:T(8,128)(2,1)S(1)}, u32[]{:S(2)}, u32[]{:S(2)}) %collective-permute-start.1) | collective-permute-done | bytes 65568 | tf_op jit(solution)/shard_map/while/body/eval_jaxpr/ppermute | solution.py:16
  196.0 3.9 collective-permute-start.1
  200.4 9.9 %collective-permute-done.1 = bf16[64,512]{1,0:T(8,128)(2,1)S(1)} collective-permute-done((bf16[64,512]{1,0:T(8,128)(2,1)S(1)}, bf16[64,512]{1,0:T(8,128)(2,1)S(1)}, u32[]{:S(2)}, u32[]{:S(2)}) %collective-permute-start.1) | collective-permute-done | bytes 65568 | tf_op jit(solution)/shard_map/while/body/eval_jaxpr/ppermute | solution.py:16
  214.0 3.9 collective-permute-start.1
  218.4 9.9 %collective-permute-done.1 = bf16[64,512]{1,0:T(8,128)(2,1)S(1)} collective-permute-done((bf16[64,512]{1,0:T(8,128)(2,1)S(1)}, bf16[64,512]{1,0:T(8,128)(2,1)S(1)}, u32[]{:S(2)}, u32[]{:S(2)}) %collective-permute-start.1) | collective-permute-done | bytes 65568 | tf_op jit(solution)/shard_map/while/body/eval_jaxpr/ppermute | solution.py:16
  232.0 3.9 collective-permute-start.1
  236.5 9.9 %collective-permute-done.1 = bf16[64,512]{1,0:T(8,128)(2,1)S(1)} collective-permute-done((bf16[64,512]{1,0:T(8,128)(2,1)S(1)}, bf16[64,512]{1,0:T(8,128)(2,1)S(1)}, u32[]{:S(2)}, u32[]{:S(2)}) %collective-permute-start.1) | collective-permute-done | bytes 65568 | tf_op jit(solution)/shard_map/while/body/eval_jaxpr/ppermute | solution.py:16
  250.1 3.9 collective-permute-start.1
  254.5 9.9 %collective-permute-done.1 = bf16[64,512]{1,0:T(8,128)(2,1)S(1)} collective-permute-done((bf16[64,512]{1,0:T(8,128)(2,1)S(1)}, bf16[64,512]{1,0:T(8,128)(2,1)S(1)}, u32[]{:S(2)}, u32[]{:S(2)}) %collective-permute-start.1) | collective-permute-done | bytes 65568 | tf_op jit(solution)/shard_map/while/body/eval_jaxpr/ppermute | solution.py:16
  268.1 3.9 collective-permute-start.1
  272.5 9.9 %collective-permute-done.1 = bf16[64,512]{1,0:T(8,128)(2,1)S(1)} collective-permute-done((bf16[64,512]{1,0:T(8,128)(2,1)S(1)}, bf16[64,512]{1,0:T(8,128)(2,1)S(1)}, u32[]{:S(2)}, u32[]{:S(2)}) %collective-permute-start.1) | collective-permute-done | bytes 65568 | tf_op jit(solution)/shard_map/while/body/eval_jaxpr/ppermute | solution.py:16
  286.2 3.9 collective-permute-start.1
  290.6 9.9 %collective-permute-done.1 = bf16[64,512]{1,0:T(8,128)(2,1)S(1)} collective-permute-done((bf16[64,512]{1,0:T(8,128)(2,1)S(1)}, bf16[64,512]{1,0:T(8,128)(2,1)S(1)}, u32[]{:S(2)}, u32[]{:S(2)}) %collective-permute-start.1) | collective-permute-done | bytes 65568 | tf_op jit(solution)/shard_map/while/body/eval_jaxpr/ppermute | solution.py:16
  304.2 3.9 collective-permute-start.1
  308.6 9.9 %collective-permute-done.1 = bf16[64,512]{1,0:T(8,128)(2,1)S(1)} collective-permute-done((bf16[64,512]{1,0:T(8,128)(2,1)S(1)}, bf16[64,512]{1,0:T(8,128)(2,1)S(1)}, u32[]{:S(2)}, u32[]{:S(2)}) %collective-permute-start.1) | collective-permute-done | bytes 65568 | tf_op jit(solution)/shard_map/while/body/eval_jaxpr/ppermute | solution.py:16
  322.2 3.9 collective-permute-start.1
  326.7 9.9 %collective-permute-done.1 = bf16[64,512]{1,0:T(8,128)(2,1)S(1)} collective-permute-done((bf16[64,512]{1,0:T(8,128)(2,1)S(1)}, bf16[64,512]{1,0:T(8,128)(2,1)S(1)}, u32[]{:S(2)}, u32[]{:S(2)}) %collective-permute-start.1) | collective-permute-done | bytes 65568 | tf_op jit(solution)/shard_map/while/body/eval_jaxpr/ppermute | solution.py:16
  340.3 3.9 collective-permute-start.1
  344.7 9.9 %collective-permute-done.1 = bf16[64,512]{1,0:T(8,128)(2,1)S(1)} collective-permute-done((bf16[64,512]{1,0:T(8,128)(2,1)S(1)}, bf16[64,512]{1,0:T(8,128)(2,1)S(1)}, u32[]{:S(2)}, u32[]{:S(2)}) %collective-permute-start.1) | collective-permute-done | bytes 65568 | tf_op jit(solution)/shard_map/while/body/eval_jaxpr/ppermute | solution.py:16
  362.7 10.3 %collective-permute-done.1 = bf16[64,512]{1,0:T(8,128)(2,1)S(1)} collective-permute-done((bf16[64,512]{1,0:T(8,128)(2,1)S(1)}, bf16[64,512]{1,0:T(8,128)(2,1)S(1)}, u32[]{:S(2)}, u32[]{:S(2)}) %collective-permute-start.1) | collective-permute-done | bytes 65568 | tf_op jit(solution)/shard_map/while/body/eval_jaxpr/ppermute | solution.py:16
  381.2 9.9 %collective-permute-done.1 = bf16[64,512]{1,0:T(8,128)(2,1)S(1)} collective-permute-done((bf16[64,512]{1,0:T(8,128)(2,1)S(1)}, bf16[64,512]{1,0:T(8,128)(2,1)S(1)}, u32[]{:S(2)}, u32[]{:S(2)}) %collective-permute-start.1) | collective-permute-done | bytes 65568 | tf_op jit(solution)/shard_map/while/body/eval_jaxpr/ppermute | solution.py:16
  399.3 10.0 %collective-permute-done.1 = bf16[64,512]{1,0:T(8,128)(2,1)S(1)} collective-permute-done((bf16[64,512]{1,0:T(8,128)(2,1)S(1)}, bf16[64,512]{1,0:T(8,128)(2,1)S(1)}, u32[]{:S(2)}, u32[]{:S(2)}) %collective-permute-start.1) | collective-permute-done | bytes 65568 | tf_op jit(solution)/shard_map/while/body/eval_jaxpr/ppermute | solution.py:16
  417.4 10.0 %collective-permute-done.1 = bf16[64,512]{1,0:T(8,128)(2,1)S(1)} collective-permute-done((bf16[64,512]{1,0:T(8,128)(2,1)S(1)}, bf16[64,512]{1,0:T(8,128)(2,1)S(1)}, u32[]{:S(2)}, u32[]{:S(2)}) %collective-permute-start.1) | collective-permute-done | bytes 65568 | tf_op jit(solution)/shard_map/while/body/eval_jaxpr/ppermute | solution.py:16
  435.6 9.9 %collective-permute-done.1 = bf16[64,512]{1,0:T(8,128)(2,1)S(1)} collective-permute-done((bf16[64,512]{1,0:T(8,128)(2,1)S(1)}, bf16[64,512]{1,0:T(8,128)(2,1)S(1)}, u32[]{:S(2)}, u32[]{:S(2)}) %collective-permute-start.1) | collective-permute-done | bytes 65568 | tf_op jit(solution)/shard_map/while/body/eval_jaxpr/ppermute | solution.py:16
  (429 shorter events, 90.0 us)
Async XLA Ops:
  4.7 141.8 %all-to-all-start = ((bf16[8,2048,192]{1,2,0:T(8,128)(2,1)}), bf16[8,2048,192]{1,2,0:T(8,128)(2,1)}, u32[]{:S(2)}, u32[]{:S(2)}) async-start(bf16[8,2048,192]{1,2,0:T(8,128)(2,1)} %stack.2), calls=%async_computation | async-start | bytes 12582912 | tf_op jit(solution)/shard_map/all_to_all | solution.py:51
  153.3 21.4 %collective-permute-start = (bf16[128,512]{0,1:T(8,128)(2,1)S(1)}, bf16[128,512]{0,1:T(8,128)(2,1)S(1)}, u32[]{:S(2)}, u32[]{:S(2)}) collective-permute-start(bf16[128,512]{0,1:T(8,128)(2,1)S(1)} %get-tuple-element.555), channel_id=1, source_target_pairs={{1,0},{2,1},{3,2},{4,3},{5,4},{6,5},{7,6},{8,7},{9,8},{10,9},{11,1... | collective-permute-start | bytes 393224 | tf_op jit(solution)/shard_map/while/body/eval_jaxpr/ppermute | solution.py:16
  159.9 14.3 %collective-permute-start.1 = (bf16[64,512]{1,0:T(8,128)(2,1)S(1)}, bf16[64,512]{1,0:T(8,128)(2,1)S(1)}, u32[]{:S(2)}, u32[]{:S(2)}) collective-permute-start(bf16[64,512]{1,0:T(8,128)(2,1)S(1)} %get-tuple-element.554), channel_id=1, source_target_pairs={{0,1},{1,2},{2,3},{3,4},{4,5},{5,6},{6,7},{7,8},{8,9},{9,10},{10,1... | collective-permute-start | bytes 196616 | tf_op jit(solution)/shard_map/while/body/eval_jaxpr/ppermute | solution.py:16
  176.0 16.7 %collective-permute-start = (bf16[128,512]{0,1:T(8,128)(2,1)S(1)}, bf16[128,512]{0,1:T(8,128)(2,1)S(1)}, u32[]{:S(2)}, u32[]{:S(2)}) collective-permute-start(bf16[128,512]{0,1:T(8,128)(2,1)S(1)} %get-tuple-element.555), channel_id=1, source_target_pairs={{1,0},{2,1},{3,2},{4,3},{5,4},{6,5},{7,6},{8,7},{9,8},{10,9},{11,1... | collective-permute-start | bytes 393224 | tf_op jit(solution)/shard_map/while/body/eval_jaxpr/ppermute | solution.py:16
  177.9 14.3 %collective-permute-start.1 = (bf16[64,512]{1,0:T(8,128)(2,1)S(1)}, bf16[64,512]{1,0:T(8,128)(2,1)S(1)}, u32[]{:S(2)}, u32[]{:S(2)}) collective-permute-start(bf16[64,512]{1,0:T(8,128)(2,1)S(1)} %get-tuple-element.554), channel_id=1, source_target_pairs={{0,1},{1,2},{2,3},{3,4},{4,5},{5,6},{6,7},{7,8},{8,9},{9,10},{10,1... | collective-permute-start | bytes 196616 | tf_op jit(solution)/shard_map/while/body/eval_jaxpr/ppermute | solution.py:16
  194.0 16.7 %collective-permute-start = (bf16[128,512]{0,1:T(8,128)(2,1)S(1)}, bf16[128,512]{0,1:T(8,128)(2,1)S(1)}, u32[]{:S(2)}, u32[]{:S(2)}) collective-permute-start(bf16[128,512]{0,1:T(8,128)(2,1)S(1)} %get-tuple-element.555), channel_id=1, source_target_pairs={{1,0},{2,1},{3,2},{4,3},{5,4},{6,5},{7,6},{8,7},{9,8},{10,9},{11,1... | collective-permute-start | bytes 393224 | tf_op jit(solution)/shard_map/while/body/eval_jaxpr/ppermute | solution.py:16
  196.0 14.3 %collective-permute-start.1 = (bf16[64,512]{1,0:T(8,128)(2,1)S(1)}, bf16[64,512]{1,0:T(8,128)(2,1)S(1)}, u32[]{:S(2)}, u32[]{:S(2)}) collective-permute-start(bf16[64,512]{1,0:T(8,128)(2,1)S(1)} %get-tuple-element.554), channel_id=1, source_target_pairs={{0,1},{1,2},{2,3},{3,4},{4,5},{5,6},{6,7},{7,8},{8,9},{9,10},{10,1... | collective-permute-start | bytes 196616 | tf_op jit(solution)/shard_map/while/body/eval_jaxpr/ppermute | solution.py:16
  212.1 16.7 %collective-permute-start = (bf16[128,512]{0,1:T(8,128)(2,1)S(1)}, bf16[128,512]{0,1:T(8,128)(2,1)S(1)}, u32[]{:S(2)}, u32[]{:S(2)}) collective-permute-start(bf16[128,512]{0,1:T(8,128)(2,1)S(1)} %get-tuple-element.555), channel_id=1, source_target_pairs={{1,0},{2,1},{3,2},{4,3},{5,4},{6,5},{7,6},{8,7},{9,8},{10,9},{11,1... | collective-permute-start | bytes 393224 | tf_op jit(solution)/shard_map/while/body/eval_jaxpr/ppermute | solution.py:16
  214.0 14.3 %collective-permute-start.1 = (bf16[64,512]{1,0:T(8,128)(2,1)S(1)}, bf16[64,512]{1,0:T(8,128)(2,1)S(1)}, u32[]{:S(2)}, u32[]{:S(2)}) collective-permute-start(bf16[64,512]{1,0:T(8,128)(2,1)S(1)} %get-tuple-element.554), channel_id=1, source_target_pairs={{0,1},{1,2},{2,3},{3,4},{4,5},{5,6},{6,7},{7,8},{8,9},{9,10},{10,1... | collective-permute-start | bytes 196616 | tf_op jit(solution)/shard_map/while/body/eval_jaxpr/ppermute | solution.py:16
  230.1 16.7 %collective-permute-start = (bf16[128,512]{0,1:T(8,128)(2,1)S(1)}, bf16[128,512]{0,1:T(8,128)(2,1)S(1)}, u32[]{:S(2)}, u32[]{:S(2)}) collective-permute-start(bf16[128,512]{0,1:T(8,128)(2,1)S(1)} %get-tuple-element.555), channel_id=1, source_target_pairs={{1,0},{2,1},{3,2},{4,3},{5,4},{6,5},{7,6},{8,7},{9,8},{10,9},{11,1... | collective-permute-start | bytes 393224 | tf_op jit(solution)/shard_map/while/body/eval_jaxpr/ppermute | solution.py:16
  232.0 14.3 %collective-permute-start.1 = (bf16[64,512]{1,0:T(8,128)(2,1)S(1)}, bf16[64,512]{1,0:T(8,128)(2,1)S(1)}, u32[]{:S(2)}, u32[]{:S(2)}) collective-permute-start(bf16[64,512]{1,0:T(8,128)(2,1)S(1)} %get-tuple-element.554), channel_id=1, source_target_pairs={{0,1},{1,2},{2,3},{3,4},{4,5},{5,6},{6,7},{7,8},{8,9},{9,10},{10,1... | collective-permute-start | bytes 196616 | tf_op jit(solution)/shard_map/while/body/eval_jaxpr/ppermute | solution.py:16
  248.1 16.7 %collective-permute-start = (bf16[128,512]{0,1:T(8,128)(2,1)S(1)}, bf16[128,512]{0,1:T(8,128)(2,1)S(1)}, u32[]{:S(2)}, u32[]{:S(2)}) collective-permute-start(bf16[128,512]{0,1:T(8,128)(2,1)S(1)} %get-tuple-element.555), channel_id=1, source_target_pairs={{1,0},{2,1},{3,2},{4,3},{5,4},{6,5},{7,6},{8,7},{9,8},{10,9},{11,1... | collective-permute-start | bytes 393224 | tf_op jit(solution)/shard_map/while/body/eval_jaxpr/ppermute | solution.py:16
  250.1 14.3 %collective-permute-start.1 = (bf16[64,512]{1,0:T(8,128)(2,1)S(1)}, bf16[64,512]{1,0:T(8,128)(2,1)S(1)}, u32[]{:S(2)}, u32[]{:S(2)}) collective-permute-start(bf16[64,512]{1,0:T(8,128)(2,1)S(1)} %get-tuple-element.554), channel_id=1, source_target_pairs={{0,1},{1,2},{2,3},{3,4},{4,5},{5,6},{6,7},{7,8},{8,9},{9,10},{10,1... | collective-permute-start | bytes 196616 | tf_op jit(solution)/shard_map/while/body/eval_jaxpr/ppermute | solution.py:16
  266.2 16.7 %collective-permute-start = (bf16[128,512]{0,1:T(8,128)(2,1)S(1)}, bf16[128,512]{0,1:T(8,128)(2,1)S(1)}, u32[]{:S(2)}, u32[]{:S(2)}) collective-permute-start(bf16[128,512]{0,1:T(8,128)(2,1)S(1)} %get-tuple-element.555), channel_id=1, source_target_pairs={{1,0},{2,1},{3,2},{4,3},{5,4},{6,5},{7,6},{8,7},{9,8},{10,9},{11,1... | collective-permute-start | bytes 393224 | tf_op jit(solution)/shard_map/while/body/eval_jaxpr/ppermute | solution.py:16
  268.1 14.3 %collective-permute-start.1 = (bf16[64,512]{1,0:T(8,128)(2,1)S(1)}, bf16[64,512]{1,0:T(8,128)(2,1)S(1)}, u32[]{:S(2)}, u32[]{:S(2)}) collective-permute-start(bf16[64,512]{1,0:T(8,128)(2,1)S(1)} %get-tuple-element.554), channel_id=1, source_target_pairs={{0,1},{1,2},{2,3},{3,4},{4,5},{5,6},{6,7},{7,8},{8,9},{9,10},{10,1... | collective-permute-start | bytes 196616 | tf_op jit(solution)/shard_map/while/body/eval_jaxpr/ppermute | solution.py:16
  284.2 16.7 %collective-permute-start = (bf16[128,512]{0,1:T(8,128)(2,1)S(1)}, bf16[128,512]{0,1:T(8,128)(2,1)S(1)}, u32[]{:S(2)}, u32[]{:S(2)}) collective-permute-start(bf16[128,512]{0,1:T(8,128)(2,1)S(1)} %get-tuple-element.555), channel_id=1, source_target_pairs={{1,0},{2,1},{3,2},{4,3},{5,4},{6,5},{7,6},{8,7},{9,8},{10,9},{11,1... | collective-permute-start | bytes 393224 | tf_op jit(solution)/shard_map/while/body/eval_jaxpr/ppermute | solution.py:16
  286.2 14.3 %collective-permute-start.1 = (bf16[64,512]{1,0:T(8,128)(2,1)S(1)}, bf16[64,512]{1,0:T(8,128)(2,1)S(1)}, u32[]{:S(2)}, u32[]{:S(2)}) collective-permute-start(bf16[64,512]{1,0:T(8,128)(2,1)S(1)} %get-tuple-element.554), channel_id=1, source_target_pairs={{0,1},{1,2},{2,3},{3,4},{4,5},{5,6},{6,7},{7,8},{8,9},{9,10},{10,1... | collective-permute-start | bytes 196616 | tf_op jit(solution)/shard_map/while/body/eval_jaxpr/ppermute | solution.py:16
  302.3 16.7 %collective-permute-start = (bf16[128,512]{0,1:T(8,128)(2,1)S(1)}, bf16[128,512]{0,1:T(8,128)(2,1)S(1)}, u32[]{:S(2)}, u32[]{:S(2)}) collective-permute-start(bf16[128,512]{0,1:T(8,128)(2,1)S(1)} %get-tuple-element.555), channel_id=1, source_target_pairs={{1,0},{2,1},{3,2},{4,3},{5,4},{6,5},{7,6},{8,7},{9,8},{10,9},{11,1... | collective-permute-start | bytes 393224 | tf_op jit(solution)/shard_map/while/body/eval_jaxpr/ppermute | solution.py:16
  304.2 14.3 %collective-permute-start.1 = (bf16[64,512]{1,0:T(8,128)(2,1)S(1)}, bf16[64,512]{1,0:T(8,128)(2,1)S(1)}, u32[]{:S(2)}, u32[]{:S(2)}) collective-permute-start(bf16[64,512]{1,0:T(8,128)(2,1)S(1)} %get-tuple-element.554), channel_id=1, source_target_pairs={{0,1},{1,2},{2,3},{3,4},{4,5},{5,6},{6,7},{7,8},{8,9},{9,10},{10,1... | collective-permute-start | bytes 196616 | tf_op jit(solution)/shard_map/while/body/eval_jaxpr/ppermute | solution.py:16
  320.3 16.7 %collective-permute-start = (bf16[128,512]{0,1:T(8,128)(2,1)S(1)}, bf16[128,512]{0,1:T(8,128)(2,1)S(1)}, u32[]{:S(2)}, u32[]{:S(2)}) collective-permute-start(bf16[128,512]{0,1:T(8,128)(2,1)S(1)} %get-tuple-element.555), channel_id=1, source_target_pairs={{1,0},{2,1},{3,2},{4,3},{5,4},{6,5},{7,6},{8,7},{9,8},{10,9},{11,1... | collective-permute-start | bytes 393224 | tf_op jit(solution)/shard_map/while/body/eval_jaxpr/ppermute | solution.py:16
  322.2 14.3 %collective-permute-start.1 = (bf16[64,512]{1,0:T(8,128)(2,1)S(1)}, bf16[64,512]{1,0:T(8,128)(2,1)S(1)}, u32[]{:S(2)}, u32[]{:S(2)}) collective-permute-start(bf16[64,512]{1,0:T(8,128)(2,1)S(1)} %get-tuple-element.554), channel_id=1, source_target_pairs={{0,1},{1,2},{2,3},{3,4},{4,5},{5,6},{6,7},{7,8},{8,9},{9,10},{10,1... | collective-permute-start | bytes 196616 | tf_op jit(solution)/shard_map/while/body/eval_jaxpr/ppermute | solution.py:16
  338.3 16.7 %collective-permute-start = (bf16[128,512]{0,1:T(8,128)(2,1)S(1)}, bf16[128,512]{0,1:T(8,128)(2,1)S(1)}, u32[]{:S(2)}, u32[]{:S(2)}) collective-permute-start(bf16[128,512]{0,1:T(8,128)(2,1)S(1)} %get-tuple-element.555), channel_id=1, source_target_pairs={{1,0},{2,1},{3,2},{4,3},{5,4},{6,5},{7,6},{8,7},{9,8},{10,9},{11,1... | collective-permute-start | bytes 393224 | tf_op jit(solution)/shard_map/while/body/eval_jaxpr/ppermute | solution.py:16
  340.3 14.3 %collective-permute-start.1 = (bf16[64,512]{1,0:T(8,128)(2,1)S(1)}, bf16[64,512]{1,0:T(8,128)(2,1)S(1)}, u32[]{:S(2)}, u32[]{:S(2)}) collective-permute-start(bf16[64,512]{1,0:T(8,128)(2,1)S(1)} %get-tuple-element.554), channel_id=1, source_target_pairs={{0,1},{1,2},{2,3},{3,4},{4,5},{5,6},{6,7},{7,8},{8,9},{9,10},{10,1... | collective-permute-start | bytes 196616 | tf_op jit(solution)/shard_map/while/body/eval_jaxpr/ppermute | solution.py:16
  356.4 17.1 %collective-permute-start = (bf16[128,512]{0,1:T(8,128)(2,1)S(1)}, bf16[128,512]{0,1:T(8,128)(2,1)S(1)}, u32[]{:S(2)}, u32[]{:S(2)}) collective-permute-start(bf16[128,512]{0,1:T(8,128)(2,1)S(1)} %get-tuple-element.555), channel_id=1, source_target_pairs={{1,0},{2,1},{3,2},{4,3},{5,4},{6,5},{7,6},{8,7},{9,8},{10,9},{11,1... | collective-permute-start | bytes 393224 | tf_op jit(solution)/shard_map/while/body/eval_jaxpr/ppermute | solution.py:16
  358.3 14.7 %collective-permute-start.1 = (bf16[64,512]{1,0:T(8,128)(2,1)S(1)}, bf16[64,512]{1,0:T(8,128)(2,1)S(1)}, u32[]{:S(2)}, u32[]{:S(2)}) collective-permute-start(bf16[64,512]{1,0:T(8,128)(2,1)S(1)} %get-tuple-element.554), channel_id=1, source_target_pairs={{0,1},{1,2},{2,3},{3,4},{4,5},{5,6},{6,7},{7,8},{8,9},{9,10},{10,1... | collective-permute-start | bytes 196616 | tf_op jit(solution)/shard_map/while/body/eval_jaxpr/ppermute | solution.py:16
  374.9 16.7 %collective-permute-start = (bf16[128,512]{0,1:T(8,128)(2,1)S(1)}, bf16[128,512]{0,1:T(8,128)(2,1)S(1)}, u32[]{:S(2)}, u32[]{:S(2)}) collective-permute-start(bf16[128,512]{0,1:T(8,128)(2,1)S(1)} %get-tuple-element.555), channel_id=1, source_target_pairs={{1,0},{2,1},{3,2},{4,3},{5,4},{6,5},{7,6},{8,7},{9,8},{10,9},{11,1... | collective-permute-start | bytes 393224 | tf_op jit(solution)/shard_map/while/body/eval_jaxpr/ppermute | solution.py:16
  376.8 14.3 %collective-permute-start.1 = (bf16[64,512]{1,0:T(8,128)(2,1)S(1)}, bf16[64,512]{1,0:T(8,128)(2,1)S(1)}, u32[]{:S(2)}, u32[]{:S(2)}) collective-permute-start(bf16[64,512]{1,0:T(8,128)(2,1)S(1)} %get-tuple-element.554), channel_id=1, source_target_pairs={{0,1},{1,2},{2,3},{3,4},{4,5},{5,6},{6,7},{7,8},{8,9},{9,10},{10,1... | collective-permute-start | bytes 196616 | tf_op jit(solution)/shard_map/while/body/eval_jaxpr/ppermute | solution.py:16
  392.9 16.8 %collective-permute-start = (bf16[128,512]{0,1:T(8,128)(2,1)S(1)}, bf16[128,512]{0,1:T(8,128)(2,1)S(1)}, u32[]{:S(2)}, u32[]{:S(2)}) collective-permute-start(bf16[128,512]{0,1:T(8,128)(2,1)S(1)} %get-tuple-element.555), channel_id=1, source_target_pairs={{1,0},{2,1},{3,2},{4,3},{5,4},{6,5},{7,6},{8,7},{9,8},{10,9},{11,1... | collective-permute-start | bytes 393224 | tf_op jit(solution)/shard_map/while/body/eval_jaxpr/ppermute | solution.py:16
  394.8 14.4 %collective-permute-start.1 = (bf16[64,512]{1,0:T(8,128)(2,1)S(1)}, bf16[64,512]{1,0:T(8,128)(2,1)S(1)}, u32[]{:S(2)}, u32[]{:S(2)}) collective-permute-start(bf16[64,512]{1,0:T(8,128)(2,1)S(1)} %get-tuple-element.554), channel_id=1, source_target_pairs={{0,1},{1,2},{2,3},{3,4},{4,5},{5,6},{6,7},{7,8},{8,9},{9,10},{10,1... | collective-permute-start | bytes 196616 | tf_op jit(solution)/shard_map/while/body/eval_jaxpr/ppermute | solution.py:16
  411.0 16.8 %collective-permute-start = (bf16[128,512]{0,1:T(8,128)(2,1)S(1)}, bf16[128,512]{0,1:T(8,128)(2,1)S(1)}, u32[]{:S(2)}, u32[]{:S(2)}) collective-permute-start(bf16[128,512]{0,1:T(8,128)(2,1)S(1)} %get-tuple-element.555), channel_id=1, source_target_pairs={{1,0},{2,1},{3,2},{4,3},{5,4},{6,5},{7,6},{8,7},{9,8},{10,9},{11,1... | collective-permute-start | bytes 393224 | tf_op jit(solution)/shard_map/while/body/eval_jaxpr/ppermute | solution.py:16
  413.0 14.4 %collective-permute-start.1 = (bf16[64,512]{1,0:T(8,128)(2,1)S(1)}, bf16[64,512]{1,0:T(8,128)(2,1)S(1)}, u32[]{:S(2)}, u32[]{:S(2)}) collective-permute-start(bf16[64,512]{1,0:T(8,128)(2,1)S(1)} %get-tuple-element.554), channel_id=1, source_target_pairs={{0,1},{1,2},{2,3},{3,4},{4,5},{5,6},{6,7},{7,8},{8,9},{9,10},{10,1... | collective-permute-start | bytes 196616 | tf_op jit(solution)/shard_map/while/body/eval_jaxpr/ppermute | solution.py:16
  429.2 16.7 %collective-permute-start = (bf16[128,512]{0,1:T(8,128)(2,1)S(1)}, bf16[128,512]{0,1:T(8,128)(2,1)S(1)}, u32[]{:S(2)}, u32[]{:S(2)}) collective-permute-start(bf16[128,512]{0,1:T(8,128)(2,1)S(1)} %get-tuple-element.555), channel_id=1, source_target_pairs={{1,0},{2,1},{3,2},{4,3},{5,4},{6,5},{7,6},{8,7},{9,8},{10,9},{11,1... | collective-permute-start | bytes 393224 | tf_op jit(solution)/shard_map/while/body/eval_jaxpr/ppermute | solution.py:16
  (4 other events, 171.5 us)
